TPU v7x, 512 devices: a whole 4x8x8 slice. The times are simulated.
512 devices in a mesh: seq: 64 (over z, y), chan: 8 (over x, core).
Axes of the slice: x: 4, y: 8, z: 8, core: 2. Of those that a mesh axis runs over, the one named last changes fastest.
Arguments:
- tokens: bfloat16 [8192, 4096], P('seq', 'chan'), may hold values from -6 to 6
- conv_taps: float32 [4, 4096], P(None, 'chan'), may hold values from -12 to 12
- log_rate: float32 [4096], P('chan'), may hold values from 4.8828125e-06 to 0.034
- rotation: float32 [4096], P('chan'), may hold values from 0 to 0.2
- in_proj: bfloat16 [64, 64, 128], P('chan'), may hold values from -0.75 to 0.75
- out_proj: bfloat16 [64, 64, 128], P('chan'), may hold values from -0.5 to 0.5
- skip_gain: float32 [4096], P('chan'), may hold values from 0.25 to 1.5
- norm_gain: float32 [4096], P('chan'), may hold values from 0.25 to 1.75
- retention: float32 [8192], P('seq'), may hold values from 0.5 to 1
- cotangent: bfloat16 [8192, 4096], P('seq', 'chan'), may hold values from -6 to 6
Outputs:
- normed: bfloat16 [8192, 4096], P('seq', 'chan')
- tokens_grad: bfloat16 [8192, 4096], P('seq', 'chan')
- in_grad: float32 [64, 64, 128], P('chan')
- out_grad: float32 [64, 64, 128], P('chan')
- taps_grad: float32 [4, 4096], P(None, 'chan')
All inputs are finite; a program needn't handle non-finite values.
Results may differ from a plain program's by a relative error of at most 0.011.
Values may be sent and summed in bfloat16 or wider, within the bound.
No kernel may reach another device: no remote copies, remote signals or barrier semaphores. Data moves between devices by JAX's collectives and lax.ppermute only.
A program may use at most 64 MiB of HBM per device.

v0:
```python
import jax
import jax.numpy as jnp
from jax import lax
from jax.sharding import Mesh, PartitionSpec as P

SEQ = ("z", "y")


def from_behind(value, axis, by):
    length = lax.axis_size(axis)
    pairs = [(i, i + by) for i in range(length) if 0 <= i + by < length]
    return lax.ppermute(value, axis, pairs)


def carried_in(part, axis, combine, identity, reverse):
    count = lax.axis_size(axis)
    place = lax.axis_index(axis)
    ahead = count - 1 - place if reverse else place
    step = -1 if reverse else 1
    packed = jnp.stack(part)
    unit = jnp.stack([jnp.zeros_like(a) + jnp.asarray(e, a.dtype) for a, e in zip(part, identity)])
    state = jnp.where(ahead >= 1, from_behind(packed, axis, step), unit)
    reach = 1
    while reach < count:
        earlier = from_behind(state, axis, step * reach)
        joined = jnp.stack(combine(tuple(earlier), tuple(state)))
        state = jnp.where(ahead >= reach, joined, state)
        reach *= 2
    return tuple(state)


def linear_run(drive_re, drive_im, decay_rate, turn_rate, log_keep):
    seq_len, num_cols = drive_re.shape
    block_len = min(64, seq_len)
    block_count = seq_len // block_len
    offsets = jnp.arange(block_len, dtype=jnp.float32)
    keep_cum = jnp.cumsum(log_keep.reshape(block_count, block_len), axis=1)[:, :, None]
    angles = offsets[:, None] * turn_rate[None, :]
    cosine = jnp.cos(angles)
    sine = jnp.sin(angles)
    growth = jnp.exp(offsets[None, :, None] * decay_rate[None, None, :] - keep_cum)
    blk_re = drive_re.reshape(block_count, block_len, num_cols)
    blk_im = drive_im.reshape(block_count, block_len, num_cols)
    pre_re = growth * (blk_re * cosine + blk_im * sine)
    pre_im = growth * (blk_im * cosine - blk_re * sine)
    lower_ones = (offsets[:, None] >= offsets[None, :]).astype(jnp.float32)
    summed = jnp.einsum(
        "ji,abik->abjk", lower_ones, jnp.stack([pre_re, pre_im]), precision=lax.Precision.HIGHEST
    )
    shrink = jnp.exp(keep_cum - offsets[None, :, None] * decay_rate[None, None, :])
    state_re = shrink * (summed[0] * cosine - summed[1] * sine)
    state_im = shrink * (summed[0] * sine + summed[1] * cosine)
    step_mag = jnp.exp(keep_cum[:, -1] - block_len * decay_rate[None, :])
    step_re = step_mag * jnp.cos(block_len * turn_rate)[None, :]
    step_im = step_mag * jnp.sin(block_len * turn_rate)[None, :]

    def advance(carried, inputs):
        carry_re, carry_im = carried
        mult_re, mult_im, end_re, end_im = inputs
        next_re = mult_re * carry_re - mult_im * carry_im + end_re
        next_im = mult_re * carry_im + mult_im * carry_re + end_im
        return ((next_re, next_im), (carry_re, carry_im))

    zeros_col = jnp.zeros((num_cols,), jnp.float32)
    enter_re, enter_im = lax.scan(
        advance, (zeros_col, zeros_col), (step_re, step_im, state_re[:, -1], state_im[:, -1])
    )[1]
    ahead = offsets + 1.0
    lift = jnp.exp(keep_cum - ahead[None, :, None] * decay_rate[None, None, :])
    lift_re = lift * jnp.cos(ahead[:, None] * turn_rate[None, :])
    lift_im = lift * jnp.sin(ahead[:, None] * turn_rate[None, :])
    state_re = state_re + lift_re * enter_re[:, None] - lift_im * enter_im[:, None]
    state_im = state_im + lift_re * enter_im[:, None] + lift_im * enter_re[:, None]
    return (state_re.reshape(seq_len, num_cols), state_im.reshape(seq_len, num_cols))


def carry_combine(earlier, later):
    early_re, early_im, early_sre, early_sim = earlier
    late_re, late_im, late_sre, late_sim = later
    joined_re = early_re * late_re - early_im * late_im
    joined_im = early_re * late_im + early_im * late_re
    joined_sre = late_re * early_sre - late_im * early_sim + late_sre
    joined_sim = late_re * early_sim + late_im * early_sre + late_sim
    return (joined_re, joined_im, joined_sre, joined_sim)


def per_device(
    tokens,
    conv_taps,
    log_rate,
    rotation,
    in_proj,
    out_proj,
    skip_gain,
    norm_gain,
    retention,
    cotangent,
):
    seq_len, local_width = tokens.shape
    tap_count = conv_taps.shape[0]
    local_heads, head_width, double_state = in_proj.shape
    state_size = double_state // 2
    num_cols = local_heads * state_size
    lead_rows = from_behind(tokens[seq_len - (tap_count - 1) :], SEQ, 1)
    padded = jnp.concatenate([lead_rows, tokens], axis=0).astype(jnp.float32)
    conv_sum = conv_taps[0][None, :] * padded[tap_count - 1 :]
    for offset in range(1, tap_count):
        conv_sum = (
            conv_sum
            + conv_taps[offset][None, :]
            * padded[tap_count - 1 - offset : tap_count - 1 - offset + seq_len]
        )
    mixed_in = conv_sum.astype(jnp.bfloat16)
    by_head = mixed_in.reshape(seq_len, local_heads, head_width)
    projected = jnp.einsum("thc,hck->thk", by_head, in_proj, preferred_element_type=jnp.float32)
    in_scale = jnp.sqrt(-jnp.expm1(-2.0 * log_rate))
    drive_re = projected[:, :, :state_size].reshape(seq_len, num_cols) * in_scale
    drive_im = projected[:, :, state_size:].reshape(seq_len, num_cols) * in_scale
    log_keep = jnp.log(retention)
    state_re, state_im = linear_run(drive_re, drive_im, log_rate, rotation, log_keep)
    keep_total = jnp.sum(log_keep)
    total_mag = jnp.exp(keep_total - seq_len * log_rate)
    total_re = total_mag * jnp.cos(seq_len * rotation)
    total_im = total_mag * jnp.sin(seq_len * rotation)
    unit_ones = jnp.ones((num_cols,), jnp.float32)
    zeros_col = jnp.zeros((num_cols,), jnp.float32)
    chained = carried_in(
        (total_re, total_im, state_re[-1], state_im[-1]),
        SEQ,
        carry_combine,
        (unit_ones, zeros_col, zeros_col, zeros_col),
        False,
    )
    enter_re, enter_im = (chained[2], chained[3])
    positions = jnp.arange(seq_len, dtype=jnp.float32)
    ahead = positions + 1.0
    lift = jnp.exp(jnp.cumsum(log_keep)[:, None] - ahead[:, None] * log_rate[None, :])
    lift_re = lift * jnp.cos(ahead[:, None] * rotation[None, :])
    lift_im = lift * jnp.sin(ahead[:, None] * rotation[None, :])
    state_re = state_re + lift_re * enter_re[None, :] - lift_im * enter_im[None, :]
    state_im = state_im + lift_re * enter_im[None, :] + lift_im * enter_re[None, :]
    state_bf = jnp.concatenate(
        [
            state_re.reshape(seq_len, local_heads, state_size),
            state_im.reshape(seq_len, local_heads, state_size),
        ],
        axis=2,
    ).astype(jnp.bfloat16)
    mixed = jnp.einsum(
        "thk,hck->thc", state_bf, out_proj, preferred_element_type=jnp.float32
    ).reshape(seq_len, local_width)
    mixed = mixed + skip_gain * mixed_in.astype(jnp.float32)
    squares = jnp.sum(mixed * mixed, axis=1)
    scaled = cotangent.astype(jnp.float32) * norm_gain
    dots = jnp.sum(scaled * mixed, axis=1)
    squares = lax.psum(squares, "chan")
    model_width = local_width * lax.axis_size("chan")
    inverse = lax.rsqrt(squares / model_width + 1e-06)
    normed = (mixed * inverse[:, None] * norm_gain).astype(jnp.bfloat16)
    dots = lax.psum(dots, "chan")
    mixed_grad = inverse[:, None] * (
        scaled - mixed * (inverse * inverse * dots / model_width)[:, None]
    )
    grad_bf = mixed_grad.astype(jnp.bfloat16).reshape(seq_len, local_heads, head_width)
    state_grad = jnp.einsum("thc,hck->thk", grad_bf, out_proj, preferred_element_type=jnp.float32)
    out_grad = jnp.einsum("thc,thk->hck", grad_bf, state_bf, preferred_element_type=jnp.float32)
    out_grad = lax.psum(lax.psum(out_grad, "y"), "z")
    back_keep = jnp.concatenate([jnp.zeros((1,), jnp.float32), log_keep[::-1][:-1]])
    grad_re = state_grad[:, :, :state_size].reshape(seq_len, num_cols)[::-1]
    grad_im = state_grad[:, :, state_size:].reshape(seq_len, num_cols)[::-1]
    adj_re, adj_im = linear_run(grad_re, grad_im, log_rate, -rotation, back_keep)
    first_mag = jnp.exp(log_keep[0] - log_rate)
    cos_turn = jnp.cos(rotation)
    sin_turn = jnp.sin(rotation)
    first_re = first_mag * (cos_turn * adj_re[-1] + sin_turn * adj_im[-1])
    first_im = first_mag * (cos_turn * adj_im[-1] - sin_turn * adj_re[-1])
    back_chained = carried_in(
        (total_re, -total_im, first_re, first_im),
        SEQ,
        carry_combine,
        (unit_ones, zeros_col, zeros_col, zeros_col),
        True,
    )
    later_re, later_im = (back_chained[2], back_chained[3])
    back_lift = jnp.exp(jnp.cumsum(back_keep)[:, None] - positions[:, None] * log_rate[None, :])
    back_re = back_lift * jnp.cos(positions[:, None] * rotation[None, :])
    back_im = -back_lift * jnp.sin(positions[:, None] * rotation[None, :])
    adj_re = adj_re + back_re * later_re[None, :] - back_im * later_im[None, :]
    adj_im = adj_im + back_re * later_im[None, :] + back_im * later_re[None, :]
    adj_re = adj_re[::-1]
    adj_im = adj_im[::-1]
    drive_grad = jnp.concatenate(
        [
            (in_scale * adj_re).reshape(seq_len, local_heads, state_size),
            (in_scale * adj_im).reshape(seq_len, local_heads, state_size),
        ],
        axis=2,
    ).astype(jnp.bfloat16)
    in_grad = jnp.einsum("thc,thk->hck", by_head, drive_grad, preferred_element_type=jnp.float32)
    input_grad = jnp.einsum(
        "thk,hck->thc", drive_grad, in_proj, preferred_element_type=jnp.float32
    ).reshape(seq_len, local_width)
    input_grad = input_grad + skip_gain * mixed_grad
    trail_rows = from_behind(input_grad[: tap_count - 1], SEQ, -1)
    tail = jnp.concatenate([input_grad, trail_rows], axis=0)
    tokens_grad = conv_taps[0][None, :] * tail[:seq_len]
    for offset in range(1, tap_count):
        tokens_grad = tokens_grad + conv_taps[offset][None, :] * tail[offset : offset + seq_len]
    taps_grad = jnp.stack(
        [
            jnp.sum(
                input_grad * padded[tap_count - 1 - offset : tap_count - 1 - offset + seq_len],
                axis=0,
            )
            for offset in range(tap_count)
        ]
    )
    packed = jnp.concatenate([in_grad.reshape(-1), taps_grad.reshape(-1)])
    packed = lax.psum(lax.psum(packed, "y"), "z")
    in_grad = packed[: in_grad.size].reshape(in_grad.shape)
    taps_grad = packed[in_grad.size :].reshape(taps_grad.shape)
    return (normed, tokens_grad.astype(jnp.bfloat16), in_grad, out_grad, taps_grad)


def solution(mesh):
    seq_count, chan_count = mesh.devices.shape
    inner = 1
    while inner * inner < seq_count:
        inner *= 2
    devices = mesh.devices.reshape(seq_count // inner, inner, chan_count)
    mesh = Mesh(devices, SEQ + ("chan",))
    in_specs = (
        P(SEQ, "chan"),
        P(None, "chan"),
        P("chan"),
        P("chan"),
        P("chan", None, None),
        P("chan", None, None),
        P("chan"),
        P("chan"),
        P(SEQ),
        P(SEQ, "chan"),
    )
    out_specs = (
        P(SEQ, "chan"),
        P(SEQ, "chan"),
        P("chan", None, None),
        P("chan", None, None),
        P(None, "chan"),
    )
    return jax.shard_map(
        per_device, mesh=mesh, in_specs=in_specs, out_specs=out_specs, check_vma=False
    )
```

profile of v0, /device:TPU:2, one launch (start us, length us, event | category | flops | bytes accessed | tf_op | source)
XLA Modules:
  0.0 364.7 jit_solution(13326804845153230500)
XLA Ops:
  8.2 3.5 collective-permute-start
  14.9 1.3 fusion.68
  16.2 2.5 multiply_cosine_fusion.1
  21.0 1.0 fusion.18
  27.2 3.5 collective-permute-start.1
  30.7 1.3 collective-permute-done.1
  32.1 4.2 %collective-permute-start.2 = (f32[4,512]{1,0:T(4,128)S(1)}, f32[4,512]{1,0:T(4,128)S(1)}, u32[]{:S(2)}, u32[]{:S(2)}) collective-permute-start(f32[4,512]{1,0:T(4,128)S(1)} %broadcast_select_fusion.5), channel_id=1, source_target_pairs={{0,8},{8,16},{16,24},{24,32},{32,40},{40,48},{48,56},{56,64},{64,7... | collective-permute-start | bytes 24584 | tf_op jit(solution)/shard_map/ppermute | solution.py:12
  36.2 1.3 collective-permute-done.2
  37.6 5.7 %collective-permute-start.3 = (f32[4,512]{1,0:T(4,128)S(1)}, f32[4,512]{1,0:T(4,128)S(1)}, u32[]{:S(2)}, u32[]{:S(2)}) collective-permute-start(f32[4,512]{1,0:T(4,128)S(1)} %maximum_select_fusion), channel_id=1, source_target_pairs={{0,16},{8,24},{16,32},{24,40},{32,48},{40,56},{48,64},{56,72},{64,... | collective-permute-start | bytes 24584 | tf_op jit(solution)/shard_map/ppermute | solution.py:12
  43.4 1.3 collective-permute-done.3
  44.8 10.6 %collective-permute-start.4 = (f32[4,512]{1,0:T(4,128)S(1)}, f32[4,512]{1,0:T(4,128)S(1)}, u32[]{:S(2)}, u32[]{:S(2)}) collective-permute-start(f32[4,512]{1,0:T(4,128)S(1)} %maximum_select_fusion.1), channel_id=1, source_target_pairs={{0,32},{8,40},{16,48},{24,56},{32,64},{40,72},{48,80},{56,88},{64,... | collective-permute-start | bytes 24584 | tf_op jit(solution)/shard_map/ppermute | solution.py:12
  55.4 1.3 collective-permute-done.4
  56.8 9.1 %collective-permute-start.5 = (f32[4,512]{1,0:T(4,128)S(1)}, f32[4,512]{1,0:T(4,128)S(1)}, u32[]{:S(2)}, u32[]{:S(2)}) collective-permute-start(f32[4,512]{1,0:T(4,128)S(1)} %maximum_select_fusion.2), channel_id=1, source_target_pairs={{0,64},{8,72},{16,80},{24,88},{32,96},{40,104},{48,112},{56,120},{... | collective-permute-start | bytes 24584 | tf_op jit(solution)/shard_map/ppermute | solution.py:12
  65.9 1.3 collective-permute-done.5
  67.4 6.1 %collective-permute-start.6 = (f32[4,512]{1,0:T(4,128)S(1)}, f32[4,512]{1,0:T(4,128)S(1)}, u32[]{:S(2)}, u32[]{:S(2)}) collective-permute-start(f32[4,512]{1,0:T(4,128)S(1)} %maximum_select_fusion.3), channel_id=1, source_target_pairs={{0,128},{8,136},{16,144},{24,152},{32,160},{40,168},{48,176},{56,1... | collective-permute-start | bytes 24584 | tf_op jit(solution)/shard_map/ppermute | solution.py:12
  73.5 1.3 collective-permute-done.6
  76.1 17.7 %collective-permute-start.7 = (f32[4,512]{1,0:T(4,128)}, f32[4,512]{1,0:T(4,128)}, u32[]{:S(2)}, u32[]{:S(2)}) collective-permute-start(f32[4,512]{1,0:T(4,128)} %maximum_select_fusion.4), channel_id=1, source_target_pairs={{0,256},{8,264},{16,272},{24,280},{32,288},{40,296},{48,304},{56,3... | collective-permute-start | bytes 24584 | tf_op jit(solution)/shard_map/ppermute | solution.py:12
  97.4 1.1 sub.357
  99.4 0.9 copy.136
  100.3 0.9 copy.138
  102.5 0.9 copy.140
  108.8 1.1 squeeze.79
  109.9 0.9 copy.141
  111.7 0.9 copy.135
  113.0 0.9 multiply_subtract_fusion.7
  115.5 2.7 subtract_convert_fusion
  119.7 10.2 %all-reduce = (f32[128]{0:T(128)S(1)}, f32[128]{0:T(128)S(1)}) all-reduce(f32[128]{0:T(128)S(1)} %get-tuple-element.185, f32[128]{0:T(128)S(1)} %get-tuple-element.184), channel_id=1, replica_groups=mesh['z'=8,'y'=8,'chan'=8] {'chan'}, use_global_device_ids=true, to_apply=%region_6.7 | all-reduce | flops 256 | bytes 2048 | tf_op jit(solution)/shard_map/psum | solution.py:156
  137.2 1.3 collective-permute-start.8
  138.5 4.2 %collective-permute-done.8 = f32[4,512]{1,0:T(4,128)S(1)} collective-permute-done((f32[4,512]{1,0:T(4,128)S(1)}, f32[4,512]{1,0:T(4,128)S(1)}, u32[]{:S(2)}, u32[]{:S(2)}) %collective-permute-start.8) | collective-permute-done | bytes 8224 | tf_op jit(solution)/shard_map/ppermute | solution.py:12
  142.7 1.3 collective-permute-start.9
  144.0 4.2 %collective-permute-done.9 = f32[4,512]{1,0:T(4,128)S(1)} collective-permute-done((f32[4,512]{1,0:T(4,128)S(1)}, f32[4,512]{1,0:T(4,128)S(1)}, u32[]{:S(2)}, u32[]{:S(2)}) %collective-permute-start.9) | collective-permute-done | bytes 8224 | tf_op jit(solution)/shard_map/ppermute | solution.py:12
  148.3 1.3 collective-permute-start.10
  149.6 5.1 %collective-permute-done.10 = f32[4,512]{1,0:T(4,128)S(1)} collective-permute-done((f32[4,512]{1,0:T(4,128)S(1)}, f32[4,512]{1,0:T(4,128)S(1)}, u32[]{:S(2)}, u32[]{:S(2)}) %collective-permute-start.10) | collective-permute-done | bytes 8224 | tf_op jit(solution)/shard_map/ppermute | solution.py:12
  154.8 1.3 collective-permute-start.11
  156.1 8.1 %collective-permute-done.11 = f32[4,512]{1,0:T(4,128)S(1)} collective-permute-done((f32[4,512]{1,0:T(4,128)S(1)}, f32[4,512]{1,0:T(4,128)S(1)}, u32[]{:S(2)}, u32[]{:S(2)}) %collective-permute-start.11) | collective-permute-done | bytes 8224 | tf_op jit(solution)/shard_map/ppermute | solution.py:12
  164.3 1.3 collective-permute-start.12
  165.6 4.3 %collective-permute-done.12 = f32[4,512]{1,0:T(4,128)S(1)} collective-permute-done((f32[4,512]{1,0:T(4,128)S(1)}, f32[4,512]{1,0:T(4,128)S(1)}, u32[]{:S(2)}, u32[]{:S(2)}) %collective-permute-start.12) | collective-permute-done | bytes 8224 | tf_op jit(solution)/shard_map/ppermute | solution.py:12
  170.0 1.3 collective-permute-start.13
  172.3 4.1 %collective-permute-done.13 = f32[4,512]{1,0:T(4,128)S(1)} collective-permute-done((f32[4,512]{1,0:T(4,128)S(1)}, f32[4,512]{1,0:T(4,128)S(1)}, u32[]{:S(2)}, u32[]{:S(2)}) %collective-permute-start.13) | collective-permute-done | bytes 8224 | tf_op jit(solution)/shard_map/ppermute | solution.py:12
  176.5 1.3 collective-permute-start.14
  177.8 1.0 fusion.35
  178.8 7.2 %collective-permute-done.14 = f32[4,512]{1,0:T(4,128)S(1)} collective-permute-done((f32[4,512]{1,0:T(4,128)S(1)}, f32[4,512]{1,0:T(4,128)S(1)}, u32[]{:S(2)}, u32[]{:S(2)}) %collective-permute-start.14) | collective-permute-done | bytes 8224 | tf_op jit(solution)/shard_map/ppermute | solution.py:12
  186.7 1.1 multiply_subtract_fusion
  192.1 80.6 %all-reduce.6.cloned.1.call-done = (f32[67584]{0:T(1024)}, f32[8,64,128]{2,1,0:T(8,128)}) async-done(((f32[67584]{0:T(1024)}, f32[8,64,128]{2,1,0:T(8,128)}), (f32[67584]{0:T(1024)}, f32[8,64,128]{2,1,0:T(8,128)})) %all-reduce.6.cloned.1.call-update) | async-done | bytes 532496 | tf_op jit(solution)/shard_map/psum | solution.py:219
  272.7 1.3 collective-permute-start.15
  274.8 6.2 %collective-permute-done.15 = f32[3,512]{0,1:T(8,128)S(1)} collective-permute-done((f32[3,512]{0,1:T(8,128)S(1)}, f32[3,512]{0,1:T(8,128)S(1)}, u32[]{:S(2)}, u32[]{:S(2)}) %collective-permute-start.15) | collective-permute-done | bytes 6176 | tf_op jit(solution)/shard_map/ppermute | solution.py:12
  282.5 71.6 %all-reduce.8.cloned.1.call-done = (f32[67584]{0:T(1024)}, f32[8,64,128]{2,1,0:T(8,128)}) async-done(((f32[67584]{0:T(1024)}, f32[8,64,128]{2,1,0:T(8,128)}), (f32[67584]{0:T(1024)}, f32[8,64,128]{2,1,0:T(8,128)})) %all-reduce.8.cloned.1.call-update) | async-done | bytes 532496 | tf_op jit(solution)/shard_map/psum | solution.py:219
  354.1 1.7 slice.228
  (359 shorter events, 45.8 us)
Async XLA Ops:
  7.2 111.1 %copy-start = (bf16[8,64,128]{2,1,0:T(8,128)(2,1)S(1)}, bf16[8,64,128]{2,1,0:T(8,128)(2,1)}, u32[]{:S(2)}) copy-start(bf16[8,64,128]{2,1,0:T(8,128)(2,1)} %param.19) | copy-start | bytes 393220
  7.2 265.5 %all-reduce.6.cloned.1.call-start = ((), (), s32[]{:S(2)}) async-start(), calls=%async_computation | async-start | bytes 1064960 | tf_op jit(solution)/shard_map/psum | solution.py:219
  8.1 3.5 copy-start.88
  8.2 13.9 %collective-permute-start = (bf16[3,512]{0,1:T(8,128)(2,1)S(1)}, bf16[3,512]{0,1:T(8,128)(2,1)S(1)}, u32[]{:S(2)}, u32[]{:S(2)}) collective-permute-start(bf16[3,512]{0,1:T(8,128)(2,1)S(1)} %copy.131), channel_id=1, source_target_pairs={{0,8},{8,16},{16,24},{24,32},{32,40},{40,48},{48,56},{56,64},{64,7... | collective-permute-start | bytes 9224 | tf_op jit(solution)/shard_map/ppermute | solution.py:12
  14.2 81.8 %copy-start.72 = (f32[2,64]{1,0:T(2,128)}, f32[2,64]{1,0:T(2,128)S(1)}, u32[]{:S(2)}) copy-start(f32[2,64]{1,0:T(2,128)S(1)} %reduce.6) | copy-start | bytes 1540
  16.2 8.3 %copy-start.57 = (f32[512]{0:T(512)}, f32[512]{0:T(512)S(1)}, u32[]{:S(2)}) copy-start(f32[512]{0:T(512)S(1)} %get-tuple-element.356) | copy-start | bytes 6148
  16.2 11.0 %copy-start.59 = (f32[512]{0:T(512)}, f32[512]{0:T(512)S(1)}, u32[]{:S(2)}) copy-start(f32[512]{0:T(512)S(1)} %get-tuple-element.352) | copy-start | bytes 6148
  18.7 1.5 copy-start.14
  20.2 2.0 copy-start.49
  20.3 2.0 copy-start.51
  20.3 2.0 copy-start.53
  20.3 2.0 copy-start.55
  27.2 4.8 %collective-permute-start.1 = (f32[4,512]{1,0:T(4,128)S(1)}, f32[4,512]{1,0:T(4,128)S(1)}, u32[]{:S(2)}, u32[]{:S(2)}) collective-permute-start(f32[4,512]{1,0:T(4,128)S(1)} %fusion.48), channel_id=1, source_target_pairs={{0,8},{8,16},{16,24},{24,32},{32,40},{40,48},{48,56},{56,64},{64,7... | collective-permute-start | bytes 24584 | tf_op jit(solution)/shard_map/ppermute | solution.py:12
  32.1 5.5 %collective-permute-start.2 = (f32[4,512]{1,0:T(4,128)S(1)}, f32[4,512]{1,0:T(4,128)S(1)}, u32[]{:S(2)}, u32[]{:S(2)}) collective-permute-start(f32[4,512]{1,0:T(4,128)S(1)} %broadcast_select_fusion.5), channel_id=1, source_target_pairs={{0,8},{8,16},{16,24},{24,32},{32,40},{40,48},{48,56},{56,64},{64,7... | collective-permute-start | bytes 24584 | tf_op jit(solution)/shard_map/ppermute | solution.py:12
  37.6 7.1 %collective-permute-start.3 = (f32[4,512]{1,0:T(4,128)S(1)}, f32[4,512]{1,0:T(4,128)S(1)}, u32[]{:S(2)}, u32[]{:S(2)}) collective-permute-start(f32[4,512]{1,0:T(4,128)S(1)} %maximum_select_fusion), channel_id=1, source_target_pairs={{0,16},{8,24},{16,32},{24,40},{32,48},{40,56},{48,64},{56,72},{64,... | collective-permute-start | bytes 24584 | tf_op jit(solution)/shard_map/ppermute | solution.py:12
  44.7 30.2 %copy-start.17 = (f32[1,512]{1,0:T(1,128)}, f32[1,512]{1,0:T(1,128)S(1)}, u32[]{:S(2)}) copy-start(f32[1,512]{1,0:T(1,128)S(1)} %get-tuple-element.319) | copy-start | bytes 6148
  44.7 30.2 %copy-start.19 = (f32[1,512]{1,0:T(1,128)}, f32[1,512]{1,0:T(1,128)S(1)}, u32[]{:S(2)}) copy-start(f32[1,512]{1,0:T(1,128)S(1)} %get-tuple-element.320) | copy-start | bytes 6148
  44.7 30.2 %copy-start.21 = (f32[1,512]{1,0:T(1,128)}, f32[1,512]{1,0:T(1,128)S(1)}, u32[]{:S(2)}) copy-start(f32[1,512]{1,0:T(1,128)S(1)} %get-tuple-element.321) | copy-start | bytes 6148
  44.8 30.2 %copy-start.23 = (f32[1,512]{1,0:T(1,128)}, f32[1,512]{1,0:T(1,128)S(1)}, u32[]{:S(2)}) copy-start(f32[1,512]{1,0:T(1,128)S(1)} %get-tuple-element.322) | copy-start | bytes 6148
  44.8 11.9 %collective-permute-start.4 = (f32[4,512]{1,0:T(4,128)S(1)}, f32[4,512]{1,0:T(4,128)S(1)}, u32[]{:S(2)}, u32[]{:S(2)}) collective-permute-start(f32[4,512]{1,0:T(4,128)S(1)} %maximum_select_fusion.1), channel_id=1, source_target_pairs={{0,32},{8,40},{16,48},{24,56},{32,64},{40,72},{48,80},{56,88},{64,... | collective-permute-start | bytes 24584 | tf_op jit(solution)/shard_map/ppermute | solution.py:12
  56.7 18.2 %copy-start.29 = (f32[1,512]{1,0:T(1,128)}, f32[1,512]{1,0:T(1,128)S(1)}, u32[]{:S(2)}) copy-start(f32[1,512]{1,0:T(1,128)S(1)} %get-tuple-element.315) | copy-start | bytes 6148
  56.7 18.2 %copy-start.31 = (f32[1,512]{1,0:T(1,128)}, f32[1,512]{1,0:T(1,128)S(1)}, u32[]{:S(2)}) copy-start(f32[1,512]{1,0:T(1,128)S(1)} %get-tuple-element.316) | copy-start | bytes 6148
  56.7 18.2 %copy-start.33 = (f32[1,512]{1,0:T(1,128)}, f32[1,512]{1,0:T(1,128)S(1)}, u32[]{:S(2)}) copy-start(f32[1,512]{1,0:T(1,128)S(1)} %get-tuple-element.317) | copy-start | bytes 6148
  56.8 18.2 %copy-start.35 = (f32[1,512]{1,0:T(1,128)}, f32[1,512]{1,0:T(1,128)S(1)}, u32[]{:S(2)}) copy-start(f32[1,512]{1,0:T(1,128)S(1)} %get-tuple-element.318) | copy-start | bytes 6148
  56.8 10.5 %collective-permute-start.5 = (f32[4,512]{1,0:T(4,128)S(1)}, f32[4,512]{1,0:T(4,128)S(1)}, u32[]{:S(2)}, u32[]{:S(2)}) collective-permute-start(f32[4,512]{1,0:T(4,128)S(1)} %maximum_select_fusion.2), channel_id=1, source_target_pairs={{0,64},{8,72},{16,80},{24,88},{32,96},{40,104},{48,112},{56,120},{... | collective-permute-start | bytes 24584 | tf_op jit(solution)/shard_map/ppermute | solution.py:12
  67.3 7.7 %copy-start.41 = (f32[1,512]{1,0:T(1,128)}, f32[1,512]{1,0:T(1,128)S(1)}, u32[]{:S(2)}) copy-start(f32[1,512]{1,0:T(1,128)S(1)} %get-tuple-element.311) | copy-start | bytes 6148
  67.3 7.7 %copy-start.43 = (f32[1,512]{1,0:T(1,128)}, f32[1,512]{1,0:T(1,128)S(1)}, u32[]{:S(2)}) copy-start(f32[1,512]{1,0:T(1,128)S(1)} %get-tuple-element.312) | copy-start | bytes 6148
  67.3 7.7 %copy-start.45 = (f32[1,512]{1,0:T(1,128)}, f32[1,512]{1,0:T(1,128)S(1)}, u32[]{:S(2)}) copy-start(f32[1,512]{1,0:T(1,128)S(1)} %get-tuple-element.313) | copy-start | bytes 6148
  67.3 7.7 %copy-start.47 = (f32[1,512]{1,0:T(1,128)}, f32[1,512]{1,0:T(1,128)S(1)}, u32[]{:S(2)}) copy-start(f32[1,512]{1,0:T(1,128)S(1)} %get-tuple-element.314) | copy-start | bytes 6148
  67.4 7.4 %collective-permute-start.6 = (f32[4,512]{1,0:T(4,128)S(1)}, f32[4,512]{1,0:T(4,128)S(1)}, u32[]{:S(2)}, u32[]{:S(2)}) collective-permute-start(f32[4,512]{1,0:T(4,128)S(1)} %maximum_select_fusion.3), channel_id=1, source_target_pairs={{0,128},{8,136},{16,144},{24,152},{32,160},{40,168},{48,176},{56,1... | collective-permute-start | bytes 24584 | tf_op jit(solution)/shard_map/ppermute | solution.py:12
  76.1 36.8 %collective-permute-start.7 = (f32[4,512]{1,0:T(4,128)}, f32[4,512]{1,0:T(4,128)}, u32[]{:S(2)}, u32[]{:S(2)}) collective-permute-start(f32[4,512]{1,0:T(4,128)} %maximum_select_fusion.4), channel_id=1, source_target_pairs={{0,256},{8,264},{16,272},{24,280},{32,288},{40,296},{48,304},{56,3... | collective-permute-start | bytes 24584 | tf_op jit(solution)/shard_map/ppermute | solution.py:12
  111.7 2.2 copy-start.68
  112.6 2.3 copy-start.6
  112.6 2.3 copy-start.7
  112.7 2.3 copy-start.8
  132.1 1.7 copy-start.38
  132.1 2.7 copy-start.11
  132.1 2.7 copy-start.12
  137.2 5.5 %collective-permute-start.8 = (f32[4,512]{1,0:T(4,128)S(1)}, f32[4,512]{1,0:T(4,128)S(1)}, u32[]{:S(2)}, u32[]{:S(2)}) collective-permute-start(f32[4,512]{1,0:T(4,128)S(1)} %fusion.50), channel_id=1, source_target_pairs={{8,0},{16,8},{24,16},{32,24},{40,32},{48,40},{56,48},{64,56},{72,6... | collective-permute-start | bytes 24584 | tf_op jit(solution)/shard_map/ppermute | solution.py:12
  142.7 5.5 %collective-permute-start.9 = (f32[4,512]{1,0:T(4,128)S(1)}, f32[4,512]{1,0:T(4,128)S(1)}, u32[]{:S(2)}, u32[]{:S(2)}) collective-permute-start(f32[4,512]{1,0:T(4,128)S(1)} %broadcast_select_fusion.4), channel_id=1, source_target_pairs={{8,0},{16,8},{24,16},{32,24},{40,32},{48,40},{56,48},{64,56},{72,6... | collective-permute-start | bytes 24584 | tf_op jit(solution)/shard_map/ppermute | solution.py:12
  148.3 6.4 %collective-permute-start.10 = (f32[4,512]{1,0:T(4,128)S(1)}, f32[4,512]{1,0:T(4,128)S(1)}, u32[]{:S(2)}, u32[]{:S(2)}) collective-permute-start(f32[4,512]{1,0:T(4,128)S(1)} %maximum_select_fusion.6), channel_id=1, source_target_pairs={{16,0},{24,8},{32,16},{40,24},{48,32},{56,40},{64,48},{72,56},{80,... | collective-permute-start | bytes 24584 | tf_op jit(solution)/shard_map/ppermute | solution.py:12
  154.8 9.5 %collective-permute-start.11 = (f32[4,512]{1,0:T(4,128)S(1)}, f32[4,512]{1,0:T(4,128)S(1)}, u32[]{:S(2)}, u32[]{:S(2)}) collective-permute-start(f32[4,512]{1,0:T(4,128)S(1)} %maximum_select_fusion.7), channel_id=1, source_target_pairs={{32,0},{40,8},{48,16},{56,24},{64,32},{72,40},{80,48},{88,56},{96,... | collective-permute-start | bytes 24584 | tf_op jit(solution)/shard_map/ppermute | solution.py:12
  164.3 5.6 %collective-permute-start.12 = (f32[4,512]{1,0:T(4,128)S(1)}, f32[4,512]{1,0:T(4,128)S(1)}, u32[]{:S(2)}, u32[]{:S(2)}) collective-permute-start(f32[4,512]{1,0:T(4,128)S(1)} %maximum_select_fusion.8), channel_id=1, source_target_pairs={{64,0},{72,8},{80,16},{88,24},{96,32},{104,40},{112,48},{120,56},{... | collective-permute-start | bytes 24584 | tf_op jit(solution)/shard_map/ppermute | solution.py:12
  170.0 6.4 %collective-permute-start.13 = (f32[4,512]{1,0:T(4,128)S(1)}, f32[4,512]{1,0:T(4,128)S(1)}, u32[]{:S(2)}, u32[]{:S(2)}) collective-permute-start(f32[4,512]{1,0:T(4,128)S(1)} %maximum_select_fusion.9), channel_id=1, source_target_pairs={{128,0},{136,8},{144,16},{152,24},{160,32},{168,40},{176,48},{184,... | collective-permute-start | bytes 24584 | tf_op jit(solution)/shard_map/ppermute | solution.py:12
  176.5 9.5 %collective-permute-start.14 = (f32[4,512]{1,0:T(4,128)S(1)}, f32[4,512]{1,0:T(4,128)S(1)}, u32[]{:S(2)}, u32[]{:S(2)}) collective-permute-start(f32[4,512]{1,0:T(4,128)S(1)} %maximum_select_fusion.10), channel_id=1, source_target_pairs={{256,0},{264,8},{272,16},{280,24},{288,32},{296,40},{304,48},{312,... | collective-permute-start | bytes 24584 | tf_op jit(solution)/shard_map/ppermute | solution.py:12
  192.1 162.0 %all-reduce.8.cloned.1.call-start = ((), (), s32[]{:S(2)}) async-start(), calls=%async_computation.1 | async-start | bytes 1064960 | tf_op jit(solution)/shard_map/psum | solution.py:219
  272.7 8.3 %collective-permute-start.15 = (f32[3,512]{0,1:T(8,128)S(1)}, f32[3,512]{0,1:T(8,128)S(1)}, u32[]{:S(2)}, u32[]{:S(2)}) collective-permute-start(f32[3,512]{0,1:T(8,128)S(1)} %bitcast.248), channel_id=1, source_target_pairs={{8,0},{16,8},{24,16},{32,24},{40,32},{48,40},{56,48},{64,56},{72,6... | collective-permute-start | bytes 18440 | tf_op jit(solution)/shard_map/ppermute | solution.py:12
  354.1 3.0 copy-start.13
  (60 other events, 48.4 us)
Sparse Core Ops, SparseCore 0:
  192.2 80.4 all-reduce.5
  275.1 78.9 all-reduce.7
where the time goes:
time: 366 us; the launch traced here: 365 us
  waiting for transfers between devices  204 us (56%)
  starting transfers between devices  70.7 us (19%)
  local copies, waits for them, and re-layouts  39.3 us (11%)
  other arithmetic  21.6 us (6%)
  between operations  15.8 us (4%)
  blocking collectives  10.2 us (3%)
    psum x2, waiting for transfers between devices, per_device(): packed = lax.psum(lax.psum(packed, 'y'), 'z')  152 us
    ppermute x16, starting transfers between devices, from_behind(): return lax.ppermute(value, axis, pairs)  70.6 us
    ppermute x16, waiting for transfers between devices, from_behind(): return lax.ppermute(value, axis, pairs)  51.6 us
    unnamed x189, local copies, waits for them, and re-layouts  15.2 us
    psum x1, blocking collectives, per_device(): squares = lax.psum(squares, 'chan')  10.2 us
  transfers between devices with their start and end apart: 18, of which 16 were waited for; matrix products, arithmetic and copies ran while one was open for 8% of the time, Pallas kernels for 0%

commit v1 on v0

--- a/solution.py
+++ b/solution.py
@@ -216,7 +216,7 @@
         ]
     )
     packed = jnp.concatenate([in_grad.reshape(-1), taps_grad.reshape(-1)])
-    packed = lax.psum(lax.psum(packed, "y"), "z")
+    packed = jnp.sum(lax.all_gather(lax.psum(packed, "y"), "z"), axis=0)
     in_grad = packed[: in_grad.size].reshape(in_grad.shape)
     taps_grad = packed[in_grad.size :].reshape(taps_grad.shape)
     return (normed, tokens_grad.astype(jnp.bfloat16), in_grad, out_grad, taps_grad)

time: 366 us -> 399 us (1.090)
  waiting for transfers between devices: 204 us -> 243 us
  local copies, waits for them, and re-layouts: 39.3 us -> 26.5 us
  other arithmetic: 21.6 us -> 28.3 us
    all_gather x0 -> x1, waiting for transfers between devices: none -> 34.5 us  [per_device(): packed = jnp.sum(lax.all_gather(lax.psum(packed, 'y'), 'z'), axis=0)]
    unnamed x189 -> x191, local copies, waits for them, and re-layouts: 15.2 us -> 3.88 us
  transfers between devices with their start and end apart: 18 -> 19, of which waited for: 16 -> 17; matrix products, arithmetic and copies ran while one was open for 8% -> 9% of each run, Pallas kernels for 0% -> 0%
where the time goes in v1:
time: 399 us; the launch traced here: 398 us
  waiting for transfers between devices  243 us (61%)
  starting transfers between devices  70.7 us (18%)
  other arithmetic  28.3 us (7%)
  local copies, waits for them, and re-layouts  26.5 us (7%)
  between operations  15.8 us (4%)
  blocking collectives  10.2 us (3%)
    psum x1, waiting for transfers between devices, per_device(): packed = jnp.sum(lax.all_gather(lax.psum(packed, 'y'), 'z'), axis=0)  80.6 us
    psum x1, waiting for transfers between devices, per_device(): out_grad = lax.psum(lax.psum(out_grad, 'y'), 'z')  75.1 us
    ppermute x16, starting transfers between devices, from_behind(): return lax.ppermute(value, axis, pairs)  70.6 us
    ppermute x16, waiting for transfers between devices, from_behind(): return lax.ppermute(value, axis, pairs)  52.2 us
    all_gather x1, waiting for transfers between devices, per_device(): packed = jnp.sum(lax.all_gather(lax.psum(packed, 'y'), 'z'), axis=0)  34.5 us
    psum x1, blocking collectives, per_device(): squares = lax.psum(squares, 'chan')  10.2 us
  transfers between devices with their start and end apart: 19, of which 17 were waited for; matrix products, arithmetic and copies ran while one was open for 9% of the time, Pallas kernels for 0%

profile of v1, /device:TPU:2, one launch (start us, length us, event | category | flops | bytes accessed | tf_op | source)
XLA Modules:
  0.0 398.1 jit_solution(16781461883795200924)
XLA Ops:
  8.2 3.5 collective-permute-start
  11.7 1.8 log_bitcast_fusion
  15.1 2.0 fusion.68
  17.1 3.2 multiply_cosine_fusion.1
  22.3 1.0 fusion.18
  28.5 3.5 collective-permute-start.1
  32.0 1.3 collective-permute-done.1
  33.4 4.2 %collective-permute-start.2 = (f32[4,512]{1,0:T(4,128)S(1)}, f32[4,512]{1,0:T(4,128)S(1)}, u32[]{:S(2)}, u32[]{:S(2)}) collective-permute-start(f32[4,512]{1,0:T(4,128)S(1)} %broadcast_select_fusion.5), channel_id=1, source_target_pairs={{0,8},{8,16},{16,24},{24,32},{32,40},{40,48},{48,56},{56,64},{64,7... | collective-permute-start | bytes 24584 | tf_op jit(solution)/shard_map/ppermute | solution.py:12
  37.6 1.3 collective-permute-done.2
  39.0 5.7 %collective-permute-start.3 = (f32[4,512]{1,0:T(4,128)S(1)}, f32[4,512]{1,0:T(4,128)S(1)}, u32[]{:S(2)}, u32[]{:S(2)}) collective-permute-start(f32[4,512]{1,0:T(4,128)S(1)} %maximum_select_fusion), channel_id=1, source_target_pairs={{0,16},{8,24},{16,32},{24,40},{32,48},{40,56},{48,64},{56,72},{64,... | collective-permute-start | bytes 24584 | tf_op jit(solution)/shard_map/ppermute | solution.py:12
  44.7 1.3 collective-permute-done.3
  46.1 10.6 %collective-permute-start.4 = (f32[4,512]{1,0:T(4,128)S(1)}, f32[4,512]{1,0:T(4,128)S(1)}, u32[]{:S(2)}, u32[]{:S(2)}) collective-permute-start(f32[4,512]{1,0:T(4,128)S(1)} %maximum_select_fusion.1), channel_id=1, source_target_pairs={{0,32},{8,40},{16,48},{24,56},{32,64},{40,72},{48,80},{56,88},{64,... | collective-permute-start | bytes 24584 | tf_op jit(solution)/shard_map/ppermute | solution.py:12
  56.7 1.3 collective-permute-done.4
  58.1 9.1 %collective-permute-start.5 = (f32[4,512]{1,0:T(4,128)S(1)}, f32[4,512]{1,0:T(4,128)S(1)}, u32[]{:S(2)}, u32[]{:S(2)}) collective-permute-start(f32[4,512]{1,0:T(4,128)S(1)} %maximum_select_fusion.2), channel_id=1, source_target_pairs={{0,64},{8,72},{16,80},{24,88},{32,96},{40,104},{48,112},{56,120},{... | collective-permute-start | bytes 24584 | tf_op jit(solution)/shard_map/ppermute | solution.py:12
  67.3 1.3 collective-permute-done.5
  68.7 6.1 %collective-permute-start.6 = (f32[4,512]{1,0:T(4,128)S(1)}, f32[4,512]{1,0:T(4,128)S(1)}, u32[]{:S(2)}, u32[]{:S(2)}) collective-permute-start(f32[4,512]{1,0:T(4,128)S(1)} %maximum_select_fusion.3), channel_id=1, source_target_pairs={{0,128},{8,136},{16,144},{24,152},{32,160},{40,168},{48,176},{56,1... | collective-permute-start | bytes 24584 | tf_op jit(solution)/shard_map/ppermute | solution.py:12
  74.8 1.3 collective-permute-done.6
  76.9 17.7 %collective-permute-start.7 = (f32[4,512]{1,0:T(4,128)}, f32[4,512]{1,0:T(4,128)}, u32[]{:S(2)}, u32[]{:S(2)}) collective-permute-start(f32[4,512]{1,0:T(4,128)} %maximum_select_fusion.4), channel_id=1, source_target_pairs={{0,256},{8,264},{16,272},{24,280},{32,288},{40,296},{48,304},{56,3... | collective-permute-start | bytes 24584 | tf_op jit(solution)/shard_map/ppermute | solution.py:12
  98.1 1.1 sub.357
  101.2 0.9 copy.171
  102.3 0.9 copy.172
  107.9 1.1 squeeze.78
  109.0 1.1 squeeze.79
  113.8 2.8 subtract_convert_fusion
  117.5 10.2 %all-reduce = (f32[128]{0:T(128)S(1)}, f32[128]{0:T(128)S(1)}) all-reduce(f32[128]{0:T(128)S(1)} %get-tuple-element.190, f32[128]{0:T(128)S(1)} %get-tuple-element.189), channel_id=1, replica_groups=mesh['z'=8,'y'=8,'chan'=8] {'chan'}, use_global_device_ids=true, to_apply=%region_6.7 | all-reduce | flops 256 | bytes 2048 | tf_op jit(solution)/shard_map/psum | solution.py:156
  131.3 1.3 collective-permute-start.8
  132.6 4.2 %collective-permute-done.8 = f32[4,512]{1,0:T(4,128)S(1)} collective-permute-done((f32[4,512]{1,0:T(4,128)S(1)}, f32[4,512]{1,0:T(4,128)S(1)}, u32[]{:S(2)}, u32[]{:S(2)}) %collective-permute-start.8) | collective-permute-done | bytes 8224 | tf_op jit(solution)/shard_map/ppermute | solution.py:12
  136.9 1.3 collective-permute-start.9
  138.2 4.2 %collective-permute-done.9 = f32[4,512]{1,0:T(4,128)S(1)} collective-permute-done((f32[4,512]{1,0:T(4,128)S(1)}, f32[4,512]{1,0:T(4,128)S(1)}, u32[]{:S(2)}, u32[]{:S(2)}) %collective-permute-start.9) | collective-permute-done | bytes 8224 | tf_op jit(solution)/shard_map/ppermute | solution.py:12
  142.4 1.3 collective-permute-start.10
  143.7 5.1 %collective-permute-done.10 = f32[4,512]{1,0:T(4,128)S(1)} collective-permute-done((f32[4,512]{1,0:T(4,128)S(1)}, f32[4,512]{1,0:T(4,128)S(1)}, u32[]{:S(2)}, u32[]{:S(2)}) %collective-permute-start.10) | collective-permute-done | bytes 8224 | tf_op jit(solution)/shard_map/ppermute | solution.py:12
  148.9 1.3 collective-permute-start.11
  150.2 8.1 %collective-permute-done.11 = f32[4,512]{1,0:T(4,128)S(1)} collective-permute-done((f32[4,512]{1,0:T(4,128)S(1)}, f32[4,512]{1,0:T(4,128)S(1)}, u32[]{:S(2)}, u32[]{:S(2)}) %collective-permute-start.11) | collective-permute-done | bytes 8224 | tf_op jit(solution)/shard_map/ppermute | solution.py:12
  158.4 1.3 collective-permute-start.12
  159.7 4.3 %collective-permute-done.12 = f32[4,512]{1,0:T(4,128)S(1)} collective-permute-done((f32[4,512]{1,0:T(4,128)S(1)}, f32[4,512]{1,0:T(4,128)S(1)}, u32[]{:S(2)}, u32[]{:S(2)}) %collective-permute-start.12) | collective-permute-done | bytes 8224 | tf_op jit(solution)/shard_map/ppermute | solution.py:12
  164.1 1.3 collective-permute-start.13
  165.8 4.7 %collective-permute-done.13 = f32[4,512]{1,0:T(4,128)S(1)} collective-permute-done((f32[4,512]{1,0:T(4,128)S(1)}, f32[4,512]{1,0:T(4,128)S(1)}, u32[]{:S(2)}, u32[]{:S(2)}) %collective-permute-start.13) | collective-permute-done | bytes 8224 | tf_op jit(solution)/shard_map/ppermute | solution.py:12
  170.6 1.3 collective-permute-start.14
  171.9 1.0 fusion.35
  172.9 7.2 %collective-permute-done.14 = f32[4,512]{1,0:T(4,128)S(1)} collective-permute-done((f32[4,512]{1,0:T(4,128)S(1)}, f32[4,512]{1,0:T(4,128)S(1)}, u32[]{:S(2)}, u32[]{:S(2)}) %collective-permute-start.14) | collective-permute-done | bytes 8224 | tf_op jit(solution)/shard_map/ppermute | solution.py:12
  180.2 1.1 multiply_subtract_fusion
  184.6 80.6 %all-reduce.7.cloned.1.call-done = (f32[1,67584]{1,0:T(1,128)}, f32[8,64,128]{2,1,0:T(8,128)}) async-done(((f32[1,67584]{1,0:T(1,128)}, f32[8,64,128]{2,1,0:T(8,128)}), (f32[1,67584]{1,0:T(1,128)}, f32[8,64,128]{2,1,0:T(8,128)})) %all-reduce.7.cloned.1.call-update) | async-done | bytes 532496 | tf_op jit(solution)/shard_map/psum | solution.py:219
  265.9 1.3 collective-permute-start.15
  268.0 6.2 %collective-permute-done.15 = f32[3,512]{0,1:T(8,128)S(1)} collective-permute-done((f32[3,512]{0,1:T(8,128)S(1)}, f32[3,512]{0,1:T(8,128)S(1)}, u32[]{:S(2)}, u32[]{:S(2)}) %collective-permute-start.15) | collective-permute-done | bytes 6176 | tf_op jit(solution)/shard_map/ppermute | solution.py:12
  275.7 34.5 %all-gather.3.cloned.1.call-done = f32[8,1,67584]{2,1,0:T(1,128)} async-done(((f32[1,1,67584]{2,1,0:T(1,128)}), f32[8,1,67584]{2,1,0:T(1,128)}) %all-gather.3.cloned.1.call-update) | async-done | bytes 2162704 | tf_op jit(solution)/shard_map/all_gather | solution.py:219
  310.3 3.2 reduce_sum.79
  314.8 75.1 %all-reduce.5.cloned.1.call-done = f32[8,64,128]{2,1,0:T(8,128)} async-done(((f32[8,64,128]{2,1,0:T(8,128)}), f32[8,64,128]{2,1,0:T(8,128)}) %all-reduce.5.cloned.1.call-update) | async-done | bytes 262160 | tf_op jit(solution)/shard_map/psum | solution.py:167
  389.9 1.7 copy.255
  (365 shorter events, 36.7 us)
Async XLA Ops:
  7.2 109.4 %copy-start = (bf16[8,64,128]{2,1,0:T(8,128)(2,1)S(1)}, bf16[8,64,128]{2,1,0:T(8,128)(2,1)}, u32[]{:S(2)}) copy-start(bf16[8,64,128]{2,1,0:T(8,128)(2,1)} %param.19) | copy-start | bytes 393220
  7.2 258.0 %all-reduce.7.cloned.1.call-start = ((), (), s32[]{:S(2)}) async-start(), calls=%async_computation.2 | async-start | bytes 1064960 | tf_op jit(solution)/shard_map/psum | solution.py:219
  8.2 15.2 %collective-permute-start = (bf16[3,512]{0,1:T(8,128)(2,1)S(1)}, bf16[3,512]{0,1:T(8,128)(2,1)S(1)}, u32[]{:S(2)}, u32[]{:S(2)}) collective-permute-start(bf16[3,512]{0,1:T(8,128)(2,1)S(1)} %copy.164), channel_id=1, source_target_pairs={{0,8},{8,16},{16,24},{24,32},{32,40},{40,48},{48,56},{56,64},{64,7... | collective-permute-start | bytes 9224 | tf_op jit(solution)/shard_map/ppermute | solution.py:12
  26.2 68.3 %copy-start.3 = (f32[1,2,64,512]{3,2,1,0:T(8,128)}, f32[1,2,64,512]{3,2,1,0:T(8,128)S(1)}, u32[]{:S(2)}) copy-start(f32[1,2,64,512]{3,2,1,0:T(8,128)S(1)} %get-tuple-element.274) | copy-start | bytes 786436
  26.2 68.3 %copy-start.4 = (f32[1,2,64,512]{3,2,1,0:T(8,128)}, f32[1,2,64,512]{3,2,1,0:T(8,128)S(1)}, u32[]{:S(2)}) copy-start(f32[1,2,64,512]{3,2,1,0:T(8,128)S(1)} %get-tuple-element.271) | copy-start | bytes 786436
  26.2 69.2 %copy-start.21 = (f32[512]{0:T(512)S(1)}, f32[512]{0:T(512)}, u32[]{:S(2)}) copy-start(f32[512]{0:T(512)} %param.16) | copy-start | bytes 6148
  26.2 69.8 %copy-start.37 = (f32[512]{0:T(512)S(1)}, f32[512]{0:T(512)}, u32[]{:S(2)}) copy-start(f32[512]{0:T(512)} %param.17) | copy-start | bytes 6148
  26.2 70.5 %copy-start.74 = (f32[2,64]{1,0:T(2,128)S(1)}, f32[2,64]{1,0:T(2,128)}, u32[]{:S(2)}) copy-start(f32[2,64]{1,0:T(2,128)} %copy-done.73) | copy-start | bytes 1540
  27.6 67.5 %copy-start.1 = (f32[2,64,512]{2,1,0:T(8,128)}, f32[2,64,512]{2,1,0:T(8,128)S(1)}, u32[]{:S(2)}) copy-start(f32[2,64,512]{2,1,0:T(8,128)S(1)} %mul.1490) | copy-start | bytes 786436
  28.5 4.8 %collective-permute-start.1 = (f32[4,512]{1,0:T(4,128)S(1)}, f32[4,512]{1,0:T(4,128)S(1)}, u32[]{:S(2)}, u32[]{:S(2)}) collective-permute-start(f32[4,512]{1,0:T(4,128)S(1)} %fusion.48), channel_id=1, source_target_pairs={{0,8},{8,16},{16,24},{24,32},{32,40},{40,48},{48,56},{56,64},{64,7... | collective-permute-start | bytes 24584 | tf_op jit(solution)/shard_map/ppermute | solution.py:12
  33.4 5.5 %collective-permute-start.2 = (f32[4,512]{1,0:T(4,128)S(1)}, f32[4,512]{1,0:T(4,128)S(1)}, u32[]{:S(2)}, u32[]{:S(2)}) collective-permute-start(f32[4,512]{1,0:T(4,128)S(1)} %broadcast_select_fusion.5), channel_id=1, source_target_pairs={{0,8},{8,16},{16,24},{24,32},{32,40},{40,48},{48,56},{56,64},{64,7... | collective-permute-start | bytes 24584 | tf_op jit(solution)/shard_map/ppermute | solution.py:12
  39.0 7.1 %collective-permute-start.3 = (f32[4,512]{1,0:T(4,128)S(1)}, f32[4,512]{1,0:T(4,128)S(1)}, u32[]{:S(2)}, u32[]{:S(2)}) collective-permute-start(f32[4,512]{1,0:T(4,128)S(1)} %maximum_select_fusion), channel_id=1, source_target_pairs={{0,16},{8,24},{16,32},{24,40},{32,48},{40,56},{48,64},{56,72},{64,... | collective-permute-start | bytes 24584 | tf_op jit(solution)/shard_map/ppermute | solution.py:12
  46.1 55.0 %copy-start.13 = (f32[1,512]{1,0:T(1,128)}, f32[1,512]{1,0:T(1,128)S(1)}, u32[]{:S(2)}) copy-start(f32[1,512]{1,0:T(1,128)S(1)} %get-tuple-element.322) | copy-start | bytes 6148
  46.1 55.0 %copy-start.15 = (f32[1,512]{1,0:T(1,128)}, f32[1,512]{1,0:T(1,128)S(1)}, u32[]{:S(2)}) copy-start(f32[1,512]{1,0:T(1,128)S(1)} %get-tuple-element.323) | copy-start | bytes 6148
  46.1 54.9 %copy-start.17 = (f32[1,512]{1,0:T(1,128)}, f32[1,512]{1,0:T(1,128)S(1)}, u32[]{:S(2)}) copy-start(f32[1,512]{1,0:T(1,128)S(1)} %get-tuple-element.324) | copy-start | bytes 6148
  46.1 54.9 %copy-start.19 = (f32[1,512]{1,0:T(1,128)}, f32[1,512]{1,0:T(1,128)S(1)}, u32[]{:S(2)}) copy-start(f32[1,512]{1,0:T(1,128)S(1)} %get-tuple-element.325) | copy-start | bytes 6148
  46.1 11.9 %collective-permute-start.4 = (f32[4,512]{1,0:T(4,128)S(1)}, f32[4,512]{1,0:T(4,128)S(1)}, u32[]{:S(2)}, u32[]{:S(2)}) collective-permute-start(f32[4,512]{1,0:T(4,128)S(1)} %maximum_select_fusion.1), channel_id=1, source_target_pairs={{0,32},{8,40},{16,48},{24,56},{32,64},{40,72},{48,80},{56,88},{64,... | collective-permute-start | bytes 24584 | tf_op jit(solution)/shard_map/ppermute | solution.py:12
  58.1 43.0 %copy-start.25 = (f32[1,512]{1,0:T(1,128)}, f32[1,512]{1,0:T(1,128)S(1)}, u32[]{:S(2)}) copy-start(f32[1,512]{1,0:T(1,128)S(1)} %get-tuple-element.318) | copy-start | bytes 6148
  58.1 43.0 %copy-start.27 = (f32[1,512]{1,0:T(1,128)}, f32[1,512]{1,0:T(1,128)S(1)}, u32[]{:S(2)}) copy-start(f32[1,512]{1,0:T(1,128)S(1)} %get-tuple-element.319) | copy-start | bytes 6148
  58.1 43.0 %copy-start.29 = (f32[1,512]{1,0:T(1,128)}, f32[1,512]{1,0:T(1,128)S(1)}, u32[]{:S(2)}) copy-start(f32[1,512]{1,0:T(1,128)S(1)} %get-tuple-element.320) | copy-start | bytes 6148
  58.1 43.0 %copy-start.31 = (f32[1,512]{1,0:T(1,128)}, f32[1,512]{1,0:T(1,128)S(1)}, u32[]{:S(2)}) copy-start(f32[1,512]{1,0:T(1,128)S(1)} %get-tuple-element.321) | copy-start | bytes 6148
  58.1 10.5 %collective-permute-start.5 = (f32[4,512]{1,0:T(4,128)S(1)}, f32[4,512]{1,0:T(4,128)S(1)}, u32[]{:S(2)}, u32[]{:S(2)}) collective-permute-start(f32[4,512]{1,0:T(4,128)S(1)} %maximum_select_fusion.2), channel_id=1, source_target_pairs={{0,64},{8,72},{16,80},{24,88},{32,96},{40,104},{48,112},{56,120},{... | collective-permute-start | bytes 24584 | tf_op jit(solution)/shard_map/ppermute | solution.py:12
  68.6 32.4 %copy-start.39 = (f32[1,512]{1,0:T(1,128)}, f32[1,512]{1,0:T(1,128)S(1)}, u32[]{:S(2)}) copy-start(f32[1,512]{1,0:T(1,128)S(1)} %get-tuple-element.314) | copy-start | bytes 6148
  68.7 32.4 %copy-start.41 = (f32[1,512]{1,0:T(1,128)}, f32[1,512]{1,0:T(1,128)S(1)}, u32[]{:S(2)}) copy-start(f32[1,512]{1,0:T(1,128)S(1)} %get-tuple-element.315) | copy-start | bytes 6148
  68.7 32.4 %copy-start.43 = (f32[1,512]{1,0:T(1,128)}, f32[1,512]{1,0:T(1,128)S(1)}, u32[]{:S(2)}) copy-start(f32[1,512]{1,0:T(1,128)S(1)} %get-tuple-element.316) | copy-start | bytes 6148
  68.7 32.4 %copy-start.45 = (f32[1,512]{1,0:T(1,128)}, f32[1,512]{1,0:T(1,128)S(1)}, u32[]{:S(2)}) copy-start(f32[1,512]{1,0:T(1,128)S(1)} %get-tuple-element.317) | copy-start | bytes 6148
  68.7 7.4 %collective-permute-start.6 = (f32[4,512]{1,0:T(4,128)S(1)}, f32[4,512]{1,0:T(4,128)S(1)}, u32[]{:S(2)}, u32[]{:S(2)}) collective-permute-start(f32[4,512]{1,0:T(4,128)S(1)} %maximum_select_fusion.3), channel_id=1, source_target_pairs={{0,128},{8,136},{16,144},{24,152},{32,160},{40,168},{48,176},{56,1... | collective-permute-start | bytes 24584 | tf_op jit(solution)/shard_map/ppermute | solution.py:12
  76.2 24.9 %copy-start.63 = (f32[1,512]{1,0:T(1,128)}, f32[1,512]{1,0:T(1,128)S(1)}, u32[]{:S(2)}) copy-start(f32[1,512]{1,0:T(1,128)S(1)} %get-tuple-element.310) | copy-start | bytes 6148
  76.2 24.9 %copy-start.65 = (f32[1,512]{1,0:T(1,128)}, f32[1,512]{1,0:T(1,128)S(1)}, u32[]{:S(2)}) copy-start(f32[1,512]{1,0:T(1,128)S(1)} %get-tuple-element.311) | copy-start | bytes 6148
  76.2 24.9 %copy-start.67 = (f32[1,512]{1,0:T(1,128)}, f32[1,512]{1,0:T(1,128)S(1)}, u32[]{:S(2)}) copy-start(f32[1,512]{1,0:T(1,128)S(1)} %get-tuple-element.312) | copy-start | bytes 6148
  76.9 35.6 %collective-permute-start.7 = (f32[4,512]{1,0:T(4,128)}, f32[4,512]{1,0:T(4,128)}, u32[]{:S(2)}, u32[]{:S(2)}) collective-permute-start(f32[4,512]{1,0:T(4,128)} %maximum_select_fusion.4), channel_id=1, source_target_pairs={{0,256},{8,264},{16,272},{24,280},{32,288},{40,296},{48,304},{56,3... | collective-permute-start | bytes 24584 | tf_op jit(solution)/shard_map/ppermute | solution.py:12
  129.5 35.9 %copy-start.88 = (f32[128,1]{0,1:T(1,128)S(1)}, f32[128,1]{0,1:T(1,128)}, u32[]{:S(2)}) copy-start(f32[128,1]{0,1:T(1,128)} %get-tuple-element.371) | copy-start | bytes 1540
  129.6 50.6 %copy-start.38 = (f32[512]{0:T(512)S(1)}, f32[512]{0:T(512)}, u32[]{:S(2)}) copy-start(f32[512]{0:T(512)} %param.17) | copy-start | bytes 6148
  131.1 50.5 %copy-start.60 = (f32[512]{0:T(512)S(1)}, f32[512]{0:T(512)}, u32[]{:S(2)}) copy-start(f32[512]{0:T(512)} %copy-done.59) | copy-start | bytes 6148
  131.3 5.5 %collective-permute-start.8 = (f32[4,512]{1,0:T(4,128)S(1)}, f32[4,512]{1,0:T(4,128)S(1)}, u32[]{:S(2)}, u32[]{:S(2)}) collective-permute-start(f32[4,512]{1,0:T(4,128)S(1)} %fusion.50), channel_id=1, source_target_pairs={{8,0},{16,8},{24,16},{32,24},{40,32},{48,40},{56,48},{64,56},{72,6... | collective-permute-start | bytes 24584 | tf_op jit(solution)/shard_map/ppermute | solution.py:12
  136.9 5.5 %collective-permute-start.9 = (f32[4,512]{1,0:T(4,128)S(1)}, f32[4,512]{1,0:T(4,128)S(1)}, u32[]{:S(2)}, u32[]{:S(2)}) collective-permute-start(f32[4,512]{1,0:T(4,128)S(1)} %broadcast_select_fusion.4), channel_id=1, source_target_pairs={{8,0},{16,8},{24,16},{32,24},{40,32},{48,40},{56,48},{64,56},{72,6... | collective-permute-start | bytes 24584 | tf_op jit(solution)/shard_map/ppermute | solution.py:12
  142.4 6.4 %collective-permute-start.10 = (f32[4,512]{1,0:T(4,128)S(1)}, f32[4,512]{1,0:T(4,128)S(1)}, u32[]{:S(2)}, u32[]{:S(2)}) collective-permute-start(f32[4,512]{1,0:T(4,128)S(1)} %maximum_select_fusion.6), channel_id=1, source_target_pairs={{16,0},{24,8},{32,16},{40,24},{48,32},{56,40},{64,48},{72,56},{80,... | collective-permute-start | bytes 24584 | tf_op jit(solution)/shard_map/ppermute | solution.py:12
  148.9 9.5 %collective-permute-start.11 = (f32[4,512]{1,0:T(4,128)S(1)}, f32[4,512]{1,0:T(4,128)S(1)}, u32[]{:S(2)}, u32[]{:S(2)}) collective-permute-start(f32[4,512]{1,0:T(4,128)S(1)} %maximum_select_fusion.7), channel_id=1, source_target_pairs={{32,0},{40,8},{48,16},{56,24},{64,32},{72,40},{80,48},{88,56},{96,... | collective-permute-start | bytes 24584 | tf_op jit(solution)/shard_map/ppermute | solution.py:12
  158.4 5.6 %collective-permute-start.12 = (f32[4,512]{1,0:T(4,128)S(1)}, f32[4,512]{1,0:T(4,128)S(1)}, u32[]{:S(2)}, u32[]{:S(2)}) collective-permute-start(f32[4,512]{1,0:T(4,128)S(1)} %maximum_select_fusion.8), channel_id=1, source_target_pairs={{64,0},{72,8},{80,16},{88,24},{96,32},{104,40},{112,48},{120,56},{... | collective-permute-start | bytes 24584 | tf_op jit(solution)/shard_map/ppermute | solution.py:12
  164.1 6.4 %collective-permute-start.13 = (f32[4,512]{1,0:T(4,128)S(1)}, f32[4,512]{1,0:T(4,128)S(1)}, u32[]{:S(2)}, u32[]{:S(2)}) collective-permute-start(f32[4,512]{1,0:T(4,128)S(1)} %maximum_select_fusion.9), channel_id=1, source_target_pairs={{128,0},{136,8},{144,16},{152,24},{160,32},{168,40},{176,48},{184,... | collective-permute-start | bytes 24584 | tf_op jit(solution)/shard_map/ppermute | solution.py:12
  170.6 9.5 %collective-permute-start.14 = (f32[4,512]{1,0:T(4,128)S(1)}, f32[4,512]{1,0:T(4,128)S(1)}, u32[]{:S(2)}, u32[]{:S(2)}) collective-permute-start(f32[4,512]{1,0:T(4,128)S(1)} %maximum_select_fusion.10), channel_id=1, source_target_pairs={{256,0},{264,8},{272,16},{280,24},{288,32},{296,40},{304,48},{312,... | collective-permute-start | bytes 24584 | tf_op jit(solution)/shard_map/ppermute | solution.py:12
  183.0 91.2 %copy-start.49 = (f32[1,512]{1,0:T(1,128)S(1)}, f32[1,512]{1,0:T(1,128)}, u32[]{:S(2)}) copy-start(f32[1,512]{1,0:T(1,128)} %copy-done.47) | copy-start | bytes 6148
  183.0 91.2 %copy-start.52 = (f32[1,512]{1,0:T(1,128)S(1)}, f32[1,512]{1,0:T(1,128)}, u32[]{:S(2)}) copy-start(f32[1,512]{1,0:T(1,128)} %copy-done.50) | copy-start | bytes 6148
  183.0 91.2 %copy-start.55 = (f32[1,512]{1,0:T(1,128)S(1)}, f32[1,512]{1,0:T(1,128)}, u32[]{:S(2)}) copy-start(f32[1,512]{1,0:T(1,128)} %copy-done.53) | copy-start | bytes 6148
  183.0 91.2 %copy-start.58 = (f32[1,512]{1,0:T(1,128)S(1)}, f32[1,512]{1,0:T(1,128)}, u32[]{:S(2)}) copy-start(f32[1,512]{1,0:T(1,128)} %copy-done.56) | copy-start | bytes 6148
  184.5 125.8 %all-gather.3.cloned.1.call-start = ((), (), s32[]{:S(2)}) async-start(), calls=%async_computation.1 | async-start | bytes 2433024 | tf_op jit(solution)/shard_map/all_gather | solution.py:219
  265.2 124.7 %all-reduce.5.cloned.1.call-start = ((), (), s32[]{:S(2)}) async-start(), calls=%async_computation | async-start | bytes 524288 | tf_op jit(solution)/shard_map/psum | solution.py:167
  265.9 8.3 %collective-permute-start.15 = (f32[3,512]{0,1:T(8,128)S(1)}, f32[3,512]{0,1:T(8,128)S(1)}, u32[]{:S(2)}, u32[]{:S(2)}) collective-permute-start(f32[3,512]{0,1:T(8,128)S(1)} %bitcast.251), channel_id=1, source_target_pairs={{8,0},{16,8},{24,16},{32,24},{40,32},{48,40},{56,48},{64,56},{72,6... | collective-permute-start | bytes 18440 | tf_op jit(solution)/shard_map/ppermute | solution.py:12
  (62 other events, 213.8 us)
Sparse Core Ops, SparseCore 0:
  184.6 80.4 all-reduce.6
  267.3 42.9 all-gather.2
  312.6 77.2 all-reduce.4
